TPU v7x, 32 devices: a whole 2x2x4 slice. The times are simulated.
32 devices in a mesh: dom: 4 (over x, core), fsdp: 8 (over z, y).
Axes of the slice: x: 2, y: 2, z: 4, core: 2. Of those that a mesh axis runs over, the one named last changes fastest.
Arguments:
- acts: bfloat16 [4096, 14336], P(('dom', 'fsdp')), may hold values from -24 to 24
- cotangent: bfloat16 [4096, 4096], P(('dom', 'fsdp')), may hold values from -0.75 to 0.75
- weight: bfloat16 [14336, 4096], P(('dom', 'fsdp')), may hold values from -0.046875 to 0.046875
- moment: float32 [14336, 4096], P(('dom', 'fsdp')), may hold values from -6 to 6
- second: float32 [14336, 4096], P(('dom', 'fsdp')), may hold values from 0.3 to 3
- log_weights: float32 [4], replicated, may hold values from -1 to 1
- domain_ids: int32 [4], replicated, may hold values from 0 to 3, each once
- step_count: int32 [1], replicated, may hold values from 1 to 8
Outputs:
- new_weight: bfloat16 [14336, 4096], P(('dom', 'fsdp'))
- new_moment: float32 [14336, 4096], P(('dom', 'fsdp'))
- new_second: float32 [14336, 4096], P(('dom', 'fsdp'))
- new_domain_weights: float32 [4], replicated
All inputs are finite; a program needn't handle non-finite values.
Results may differ from a plain program's by a relative error of at most 0.001.
Values may be sent and summed in bfloat16 or wider, within the bound.
No kernel may reach another device: no remote copies, remote signals or barrier semaphores. Data moves between devices by JAX's collectives and lax.ppermute only.
A program may use at most 192 MiB of HBM per device.

v0:
```python
import jax
import jax.numpy as jnp
from jax import lax
from jax.sharding import Mesh, PartitionSpec as P

FLAT = ("x", "core", "fsdp")


def on_device(acts, cotangent, weight, moment, second, log_weights, domain_ids, step_count):
    groups = lax.axis_size("x") * lax.axis_size("core")
    devices = lax.axis_size(FLAT)
    tok_rows = acts.shape[0]
    group_tok = devices // groups * tok_rows
    width = cotangent.shape[1]
    own_rows = weight.shape[0]
    core = lax.axis_index("core")
    shaped = acts.reshape(tok_rows, devices, own_rows)
    columns = lax.all_to_all(shaped, FLAT, split_axis=1, concat_axis=0, tiled=True)
    columns = columns.reshape(groups, group_tok, own_rows)
    mine = lax.all_gather(cotangent, ("x", "fsdp"), axis=0, tiled=True)
    mine = mine.reshape(groups // 2, group_tok, width)
    theirs = lax.ppermute(mine, "core", [(0, 1), (1, 0)])
    half = jnp.arange(groups // 2, dtype=jnp.int32) * 2
    order = jnp.concatenate([half + core, half + 1 - core])
    local_cols = jnp.take(columns, order, axis=0)
    dims = (((1,), (1,)), ((0,), (0,)))
    g_mine = lax.dot_general(
        local_cols[: groups // 2], mine, dims, preferred_element_type=jnp.float32
    )
    g_theirs = lax.dot_general(
        local_cols[groups // 2 :], theirs, dims, preferred_element_type=jnp.float32
    )
    owned = jnp.concatenate([g_mine, g_theirs]).astype(jnp.bfloat16)
    pairs = {}
    for i in range(groups):
        for j in range(i, groups):
            pairs[i, j] = jnp.sum(owned[i].astype(jnp.float32) * owned[j].astype(jnp.float32))
    local_gram = jnp.stack(
        [jnp.stack([pairs[min(i, j), max(i, j)] for j in range(groups)]) for i in range(groups)]
    )
    perm = (order[:, None] == jnp.arange(groups, dtype=jnp.int32)[None, :]).astype(jnp.float32)
    device_gram = jnp.dot(
        perm.T,
        jnp.dot(local_gram, perm, precision=lax.Precision.HIGHEST),
        precision=lax.Precision.HIGHEST,
    )
    gram = lax.psum(device_gram, FLAT)
    score = jnp.sum(gram, axis=1) * (groups / jnp.trace(gram))
    onehot = (domain_ids[:, None] == jnp.arange(groups, dtype=jnp.int32)[None, :]).astype(
        jnp.float32
    )
    logits = log_weights + 2.0 * jnp.sum(onehot * score[:, None], axis=0)
    new_domain_weights = jax.nn.softmax(logits)
    group_w = jnp.sum(onehot * new_domain_weights[None, :], axis=1)
    local_w = jnp.take(group_w, order)
    combined = jnp.zeros((own_rows, width), jnp.float32)
    for group in range(groups):
        combined = combined + local_w[group] * owned[group].astype(jnp.float32)
    steps_f = step_count[0].astype(jnp.float32)
    new_moment = 0.9 * moment + 0.1 * combined
    new_second = 0.95 * second + 0.05 * combined * combined
    fix_one = 1.0 - jnp.exp(steps_f * jnp.log(jnp.float32(0.9)))
    fix_two = 1.0 - jnp.exp(steps_f * jnp.log(jnp.float32(0.95)))
    update = new_moment / fix_one / (jnp.sqrt(new_second / fix_two) + 1e-08)
    new_weight = (weight.astype(jnp.float32) - 0.002 * update).astype(jnp.bfloat16)
    return (new_weight, new_moment, new_second, new_domain_weights)


def solution(mesh):
    chips = mesh.shape["dom"] // 2
    flat = Mesh(mesh.devices.reshape(chips, 2, mesh.shape["fsdp"]), FLAT)
    row = P(FLAT, None)
    return jax.shard_map(
        on_device,
        mesh=flat,
        in_specs=(row, row, row, row, row, P(), P(), P()),
        out_specs=(row, row, row, P()),
        check_vma=False,
    )
```

profile of v0, /device:TPU:10, one launch (start us, length us, event | category | flops | bytes accessed | tf_op | source)
XLA Modules:
  0.0 442.7 jit_solution(5612027827097999883)
XLA Ops:
  7.2 0.0 all-gather.2.cloned.1.call-start
  7.2 0.7 all-gather.2.cloned.1.call-update
  7.9 193.8 %all-gather.2.cloned.1.call-done = bf16[2048,4096]{1,0:T(8,128)(2,1)} async-done(((bf16[128,4096]{1,0:T(8,128)(2,1)}), bf16[2048,4096]{1,0:T(8,128)(2,1)}) %all-gather.2.cloned.1.call-update) | async-done | bytes 16777232 | tf_op jit(solution)/shard_map/all_gather | solution.py:20
  201.7 0.0 collective-permute-start
  201.7 6.0 %copy.12 = bf16[128,14336]{0,1:T(8,128)(2,1)} copy(bf16[128,14336]{1,0:T(8,128)(2,1)} %param.8) | data formatting | bytes 7340032 | tf_op args[0]
  207.8 5.6 %all-to-all-start = ((bf16[128,32,448]{0,2,1:T(8,128)(2,1)}), bf16[128,32,448]{0,2,1:T(8,128)(2,1)}, u32[]{:S(2)}, u32[]{:S(2)}) async-start(bf16[128,32,448]{0,2,1:T(8,128)(2,1)} %bitcast.50), calls=%async_computation | async-start | bytes 7340032 | tf_op jit(solution)/shard_map/all_to_all | solution.py:18
  214.1 0.1 fusion.26
  214.2 0.1 compare_and_fusion
  214.2 79.3 %all-to-all-done = bf16[128,32,448]{0,2,1:T(8,128)(2,1)} async-done(((bf16[128,32,448]{0,2,1:T(8,128)(2,1)}), bf16[128,32,448]{0,2,1:T(8,128)(2,1)}, u32[]{:S(2)}, u32[]{:S(2)}) %all-to-all-start) | async-done | bytes 3670048 | tf_op jit(solution)/shard_map/all_to_all | solution.py:18
  293.6 6.2 %copy.13 = bf16[32,128,1,448]{1,0,3,2:T(8,128)(2,1)} copy(bf16[32,128,1,448]{1,3,0,2:T(8,128)(2,1)} %bitcast.2) | data formatting | bytes 7340032 | tf_op jit(solution)/shard_map/all_to_all | solution.py:18
  299.8 6.3 %reshape.125 = bf16[4,1024,448]{1,0,2:T(4,128)(2,1)} reshape(bf16[32,128,1,448]{1,0,3,2:T(8,128)(2,1)} %copy.13) | data formatting | bytes 7340032 | tf_op jit(solution)/shard_map/reshape | solution.py:19
  306.1 5.1 %copy.14 = bf16[4,1024,448]{1,2,0:T(8,128)(2,1)} copy(bf16[4,1024,448]{1,0,2:T(4,128)(2,1)} %reshape.125) | data formatting | bytes 7340032 | tf_op jit(solution)/shard_map/reshape | solution.py:19
  311.2 4.7 %gather_fusion = bf16[4,1024,448]{1,2,0:T(8,128)(2,1)} fusion(bf16[4,1024,448]{1,2,0:T(8,128)(2,1)} %copy.14, s32[1024]{0:T(1024)S(1)} %pad_clamp_fusion), kind=kCustom, calls=%fused_computation | custom fusion | bytes 7340048 | tf_op jit(solution)/shard_map/jit(_take)/gather | solution.py:25
  315.8 13.8 %convolution_convert_fusion.1 = bf16[2,448,4096]{2,1,0:T(8,128)(2,1)} fusion(bf16[2,1024,4096]{2,1,0:T(8,128)(2,1)} %bitcast.52, bf16[4,1024,448]{1,2,0:T(8,128)(2,1)} %gather_fusion, pred[4]{0:T(512)(128)(4,1)S(1)} %get-tuple-element.21), kind=kOutput, calls=%fused_computation.35 | convolution fusion | flops 7521697792 | bytes 27787268 | tf_op jit(solution)/shard_map/dot_general | solution.py:27
  329.6 0.0 collective-permute-done
  329.6 14.0 %convolution_convert_fusion = bf16[2,448,4096]{2,1,0:T(8,128)(2,1)} fusion(bf16[2,1024,4096]{2,1,0:T(8,128)(2,1)} %collective-permute-done, bf16[4,1024,448]{1,2,0:T(8,128)(2,1)} %gather_fusion, pred[4]{0:T(512)(128)(4,1)S(1)} %get-tuple-element.21), kind=kOutput, calls=%fused_computation.34 | convolution fusion | flops 7521697792 | bytes 27787268 | tf_op jit(solution)/shard_map/dot_general | solution.py:30
  343.6 0.0 copy-start.1
  343.6 0.0 copy-start
  343.6 9.2 %fusion.8 = (f32[]{:T(128)}, f32[]{:T(128)}, f32[]{:T(128)}, f32[]{:T(128)}, f32[]{:T(128)}, /*index=5*/f32[]{:T(128)}, f32[]{:T(128)}, f32[]{:T(128)}, f32[]{:T(128)}, f32[]{:T(128)}) fusion(bf16[2,448,4096]{2,1,0:T(8,128)(2,1)} %convolution_convert_fusion, bf16[2,448,4096]{2,1,0:T(8,128)(2,1)} %convolution_convert_fusion.1), kind=kLoop, calls=%fused_computation.25 | loop fusion | flops 44040188 | bytes 14680104 | tf_op jit(solution)/shard_map/reduce_sum | solution.py:37
  352.7 2.6 maximum_bitcast_fusion
  355.3 2.6 maximum_bitcast_fusion.1
  357.9 2.7 maximum_bitcast_fusion.2
  360.6 2.7 maximum_bitcast_fusion.3
  363.3 0.2 fusion.15
  363.5 0.3 fusion.23
  363.7 43.1 %psum.7 = f32[4,4]{1,0:T(4,128)S(1)} all-reduce(f32[4,4]{1,0:T(4,128)S(1)} %fusion.23), channel_id=1, replica_groups=mesh['x'=2,'core'=2,'fsdp'=8] {'x','core','fsdp'}, use_global_device_ids=true, to_apply=%region_10.11 | all-reduce | flops 16 | bytes 128 | tf_op jit(solution)/shard_map/psum | solution.py:47
  406.8 0.6 select_reduce_fusion.2
  408.2 0.0 copy-done.1
  408.2 0.1 select_reduce_fusion.1
  408.3 0.0 copy-done
  408.3 0.6 fusion.31
  408.9 1.3 fusion.35
  410.1 0.6 broadcast_divide_fusion
  410.8 0.0 copy-start.2
  410.8 0.2 select_reduce_fusion
  411.0 0.6 gather_fusion.1
  411.6 0.7 fusion.36
  412.3 23.5 %subtract_convert_fusion = (bf16[448,4096]{1,0:T(8,128)(2,1)}, f32[448,4096]{1,0:T(8,128)}, f32[448,4096]{1,0:T(8,128)}) fusion(bf16[448,4096]{1,0:T(8,128)(2,1)} %param.10, f32[]{:T(128)} %bitcast.27, f32[]{:T(128)} %bitcast.26, bf16[2,448,4096]{2,1,0:T(8,128)(2,1)} %convolution_convert_fusion, f32[]{:T(128)} %bitcast.24, f32[]{:T(128)} %bitcast.23, ...), kind=kLoop, calls=%fused_computation.32 | loop fusion | flops 47710208 | bytes 51380248 | tf_op jit(solution)/shard_map/convert_element_type | solution.py:65
  435.8 0.0 copy-done.2
  (5 shorter events, 0.0 us)
Async XLA Ops:
  7.2 194.5 %all-gather.2.cloned.1.call-start = ((), (), s32[]{:S(2)}) async-start(), calls=%async_computation.1 | async-start | bytes 17825792 | tf_op jit(solution)/shard_map/all_gather | solution.py:20
  201.7 127.9 %collective-permute-start = (bf16[2,1024,4096]{2,1,0:T(8,128)(2,1)}, bf16[2,1024,4096]{2,1,0:T(8,128)(2,1)}, u32[]{:S(2)}, u32[]{:S(2)}) collective-permute-start(bf16[2,1024,4096]{2,1,0:T(8,128)(2,1)} %bitcast.51), channel_id=1, source_target_pairs={{0,8},{8,0},{1,9},{9,1},{2,10},{10,2},{3,11},{11,3},{4,12},{12,4},... | collective-permute-start | bytes 50331656 | tf_op jit(solution)/shard_map/ppermute | solution.py:22
  207.8 85.8 %all-to-all-start = ((bf16[128,32,448]{0,2,1:T(8,128)(2,1)}), bf16[128,32,448]{0,2,1:T(8,128)(2,1)}, u32[]{:S(2)}, u32[]{:S(2)}) async-start(bf16[128,32,448]{0,2,1:T(8,128)(2,1)} %bitcast.50), calls=%async_computation | async-start | bytes 7340032 | tf_op jit(solution)/shard_map/all_to_all | solution.py:18
  343.6 64.6 %copy-start.1 = (s32[4]{0:T(128)S(1)}, s32[4]{0:T(128)}, u32[]{:S(2)}) copy-start(s32[4]{0:T(128)} %param.14) | copy-start | bytes 52
  343.6 64.7 %copy-start = (f32[4]{0:T(128)S(1)}, f32[4]{0:T(128)}, u32[]{:S(2)}) copy-start(f32[4]{0:T(128)} %param.13) | copy-start | bytes 52
  410.8 25.0 %copy-start.2 = (f32[4]{0:T(128)}, f32[4]{0:T(128)S(1)}, u32[]{:S(2)}) copy-start(f32[4]{0:T(128)S(1)} %broadcast_divide_fusion) | copy-start | bytes 52
Sparse Core Ops, SparseCore 0:
  10.8 190.8 all-gather.1
where the time goes:
time: 444 us; the launch traced here: 443 us
  waiting for transfers between devices  274 us (62%)
  other arithmetic  46.9 us (11%)
  blocking collectives  43.1 us (10%)
  local copies, waits for them, and re-layouts  29.6 us (7%)
  matrix products  28.2 us (6%)
  between operations  15.5 us (3%)
  starting transfers between devices  5.61 us (1%)
    all_gather x1, waiting for transfers between devices, on_device(): mine = lax.all_gather(cotangent, ('x', 'fsdp'), axis=0, tiled=True)  194 us
    all_to_all x1, waiting for transfers between devices, on_device(): lax.all_to_all(shaped, FLAT, split_axis=1, concat_axis=0, tiled=True)  79.3 us
    psum x1, blocking collectives, on_device(): gram = lax.psum(device_gram, FLAT)  43.1 us
    convert_element_type x1, other arithmetic, on_device(): (weight.astype(jnp.float32) - 0.002 * update).astype(jnp.bfloat16)  23.5 us
    dot_general x1, matrix products, on_device(): lax.dot_general(local_cols[groups // 2:], theirs, dims, preferred_element...  14 us
    dot_general x1, matrix products, on_device(): lax.dot_general(local_cols[:groups // 2], mine, dims, preferred_element_t...  13.8 us
    reshape x2, local copies, waits for them, and re-layouts, on_device(): columns = columns.reshape(groups, group_tok, own_rows)  11.3 us
    another operation x4, other arithmetic, on_device(): jnp.stack([jnp.stack([pairs[min(i, j), max(i, j)] for j in range(groups)]...  10.6 us
  transfers between devices with their start and end apart: 3, of which 2 were waited for; matrix products, arithmetic and copies ran while one was open for 10% of the time, Pallas kernels for 0%

commit v1 on v0

--- a/solution.py
+++ b/solution.py
@@ -44,7 +44,7 @@
         jnp.dot(local_gram, perm, precision=lax.Precision.HIGHEST),
         precision=lax.Precision.HIGHEST,
     )
-    gram = lax.psum(device_gram, FLAT)
+    gram = jnp.sum(lax.all_gather(device_gram, FLAT), axis=0)
     score = jnp.sum(gram, axis=1) * (groups / jnp.trace(gram))
     onehot = (domain_ids[:, None] == jnp.arange(groups, dtype=jnp.int32)[None, :]).astype(
         jnp.float32

time: 444 us -> 470 us (1.059)
  blocking collectives: 43.1 us -> 64.6 us
    all_gather x0 -> x1, blocking collectives: none -> 64.6 us  [on_device(): gram = jnp.sum(lax.all_gather(device_gram, FLAT), axis=0)]
    psum x1 -> x0, blocking collectives: 43.1 us -> none  [on_device(): gram = lax.psum(device_gram, FLAT)]
  transfers between devices with their start and end apart: 3 -> 3, of which waited for: 2 -> 2; matrix products, arithmetic and copies ran while one was open for 10% -> 9% of each run, Pallas kernels for 0% -> 0%
where the time goes in v1:
time: 470 us; the launch traced here: 464 us
  waiting for transfers between devices  274 us (58%)
  blocking collectives  64.6 us (14%)
  other arithmetic  46.9 us (10%)
  local copies, waits for them, and re-layouts  29.6 us (6%)
  matrix products  28.2 us (6%)
  between operations  15.5 us (3%)
  starting transfers between devices  5.61 us (1%)
    all_gather x1, waiting for transfers between devices, on_device(): mine = lax.all_gather(cotangent, ('x', 'fsdp'), axis=0, tiled=True)  194 us
    all_to_all x1, waiting for transfers between devices, on_device(): lax.all_to_all(shaped, FLAT, split_axis=1, concat_axis=0, tiled=True)  79.3 us
    all_gather x1, blocking collectives, on_device(): gram = jnp.sum(lax.all_gather(device_gram, FLAT), axis=0)  64.6 us
    convert_element_type x1, other arithmetic, on_device(): (weight.astype(jnp.float32) - 0.002 * update).astype(jnp.bfloat16)  23.5 us
    dot_general x1, matrix products, on_device(): lax.dot_general(local_cols[groups // 2:], theirs, dims, preferred_element...  14 us
    dot_general x1, matrix products, on_device(): lax.dot_general(local_cols[:groups // 2], mine, dims, preferred_element_t...  13.8 us
    reshape x2, local copies, waits for them, and re-layouts, on_device(): columns = columns.reshape(groups, group_tok, own_rows)  11.3 us
    another operation x4, other arithmetic, on_device(): jnp.stack([jnp.stack([pairs[min(i, j), max(i, j)] for j in range(groups)]...  10.6 us
  transfers between devices with their start and end apart: 3, of which 2 were waited for; matrix products, arithmetic and copies ran while one was open for 9% of the time, Pallas kernels for 0%

profile of v1, /device:TPU:10, one launch (start us, length us, event | category | flops | bytes accessed | tf_op | source)
XLA Modules:
  0.0 464.2 jit_solution(9218684040570246565)
XLA Ops:
  7.2 0.0 all-gather.4.cloned.1.call-start
  7.2 0.7 all-gather.4.cloned.1.call-update
  7.9 193.8 %all-gather.4.cloned.1.call-done = bf16[2048,4096]{1,0:T(8,128)(2,1)} async-done(((bf16[128,4096]{1,0:T(8,128)(2,1)}), bf16[2048,4096]{1,0:T(8,128)(2,1)}) %all-gather.4.cloned.1.call-update) | async-done | bytes 16777232 | tf_op jit(solution)/shard_map/all_gather | solution.py:20
  201.7 0.0 collective-permute-start
  201.7 6.0 %copy.18 = bf16[128,14336]{0,1:T(8,128)(2,1)} copy(bf16[128,14336]{1,0:T(8,128)(2,1)} %param.8) | data formatting | bytes 7340032 | tf_op args[0]
  207.8 5.6 %all-to-all-start = ((bf16[128,32,448]{0,2,1:T(8,128)(2,1)}), bf16[128,32,448]{0,2,1:T(8,128)(2,1)}, u32[]{:S(2)}, u32[]{:S(2)}) async-start(bf16[128,32,448]{0,2,1:T(8,128)(2,1)} %bitcast.52), calls=%async_computation | async-start | bytes 7340032 | tf_op jit(solution)/shard_map/all_to_all | solution.py:18
  214.1 0.1 fusion.25
  214.2 0.1 compare_and_fusion
  214.2 79.3 %all-to-all-done = bf16[128,32,448]{0,2,1:T(8,128)(2,1)} async-done(((bf16[128,32,448]{0,2,1:T(8,128)(2,1)}), bf16[128,32,448]{0,2,1:T(8,128)(2,1)}, u32[]{:S(2)}, u32[]{:S(2)}) %all-to-all-start) | async-done | bytes 3670048 | tf_op jit(solution)/shard_map/all_to_all | solution.py:18
  293.6 6.2 %copy.19 = bf16[32,128,1,448]{1,0,3,2:T(8,128)(2,1)} copy(bf16[32,128,1,448]{1,3,0,2:T(8,128)(2,1)} %bitcast.2) | data formatting | bytes 7340032 | tf_op jit(solution)/shard_map/all_to_all | solution.py:18
  299.8 6.3 %reshape.125 = bf16[4,1024,448]{1,0,2:T(4,128)(2,1)} reshape(bf16[32,128,1,448]{1,0,3,2:T(8,128)(2,1)} %copy.19) | data formatting | bytes 7340032 | tf_op jit(solution)/shard_map/reshape | solution.py:19
  306.1 5.1 %copy.20 = bf16[4,1024,448]{1,2,0:T(8,128)(2,1)} copy(bf16[4,1024,448]{1,0,2:T(4,128)(2,1)} %reshape.125) | data formatting | bytes 7340032 | tf_op jit(solution)/shard_map/reshape | solution.py:19
  311.2 4.7 %gather_fusion = bf16[4,1024,448]{1,2,0:T(8,128)(2,1)} fusion(bf16[4,1024,448]{1,2,0:T(8,128)(2,1)} %copy.20, s32[1024]{0:T(1024)S(1)} %pad_clamp_fusion), kind=kCustom, calls=%fused_computation | custom fusion | bytes 7340048 | tf_op jit(solution)/shard_map/jit(_take)/gather | solution.py:25
  315.8 13.8 %convolution_convert_fusion.1 = bf16[2,448,4096]{2,1,0:T(8,128)(2,1)} fusion(bf16[2,1024,4096]{2,1,0:T(8,128)(2,1)} %bitcast.54, bf16[4,1024,448]{1,2,0:T(8,128)(2,1)} %gather_fusion, pred[4]{0:T(512)(128)(4,1)S(1)} %get-tuple-element.21), kind=kOutput, calls=%fused_computation.35 | convolution fusion | flops 7521697792 | bytes 27787268 | tf_op jit(solution)/shard_map/dot_general | solution.py:27
  329.6 0.0 collective-permute-done
  329.6 14.0 %convolution_convert_fusion = bf16[2,448,4096]{2,1,0:T(8,128)(2,1)} fusion(bf16[2,1024,4096]{2,1,0:T(8,128)(2,1)} %collective-permute-done, bf16[4,1024,448]{1,2,0:T(8,128)(2,1)} %gather_fusion, pred[4]{0:T(512)(128)(4,1)S(1)} %get-tuple-element.21), kind=kOutput, calls=%fused_computation.34 | convolution fusion | flops 7521697792 | bytes 27787268 | tf_op jit(solution)/shard_map/dot_general | solution.py:30
  343.6 0.0 copy-start.1
  343.6 0.0 copy-start
  343.6 9.2 %fusion.8 = (f32[]{:T(128)}, f32[]{:T(128)}, f32[]{:T(128)}, f32[]{:T(128)}, f32[]{:T(128)}, /*index=5*/f32[]{:T(128)}, f32[]{:T(128)}, f32[]{:T(128)}, f32[]{:T(128)}, f32[]{:T(128)}) fusion(bf16[2,448,4096]{2,1,0:T(8,128)(2,1)} %convolution_convert_fusion, bf16[2,448,4096]{2,1,0:T(8,128)(2,1)} %convolution_convert_fusion.1), kind=kLoop, calls=%fused_computation.25 | loop fusion | flops 44040188 | bytes 14680104 | tf_op jit(solution)/shard_map/reduce_sum | solution.py:37
  352.7 2.6 maximum_bitcast_fusion
  355.3 2.6 maximum_bitcast_fusion.1
  357.9 2.7 maximum_bitcast_fusion.2
  360.6 2.7 maximum_bitcast_fusion.3
  363.3 0.2 fusion.15
  363.5 0.3 convolution_bitcast_fusion
  363.7 64.6 %all-gather.1 = f32[32,4,4]{2,1,0:T(4,128)S(1)} all-gather(f32[1,4,4]{2,1,0:T(4,128)S(1)} %convolution_bitcast_fusion), channel_id=2, replica_groups=mesh['x'=2,'core'=2,'fsdp'=8] {'x','core','fsdp'}, dimensions={0}, use_global_device_ids=true | all-gather | bytes 2112 | tf_op jit(solution)/shard_map/all_gather | solution.py:47
  428.3 0.1 fusion.33
  428.5 0.6 select_reduce_fusion.2
  429.8 0.0 copy-done.1
  429.8 0.1 select_reduce_fusion.1
  429.9 0.0 copy-done
  429.9 0.6 fusion.30
  430.5 1.3 fusion.35
  431.7 0.6 broadcast_divide_fusion
  432.4 0.0 copy-start.2
  432.4 0.2 select_reduce_fusion
  432.6 0.6 gather_fusion.1
  433.2 0.7 fusion.36
  433.9 23.5 %subtract_convert_fusion = (bf16[448,4096]{1,0:T(8,128)(2,1)}, f32[448,4096]{1,0:T(8,128)}, f32[448,4096]{1,0:T(8,128)}) fusion(bf16[448,4096]{1,0:T(8,128)(2,1)} %param.10, f32[]{:T(128)} %bitcast.28, f32[]{:T(128)} %bitcast.27, bf16[2,448,4096]{2,1,0:T(8,128)(2,1)} %convolution_convert_fusion, f32[]{:T(128)} %bitcast.25, f32[]{:T(128)} %bitcast.24, ...), kind=kLoop, calls=%fused_computation.32 | loop fusion | flops 47710208 | bytes 51380248 | tf_op jit(solution)/shard_map/convert_element_type | solution.py:65
  457.4 0.0 copy-done.2
  (5 shorter events, 0.0 us)
Async XLA Ops:
  7.2 194.5 %all-gather.4.cloned.1.call-start = ((), (), s32[]{:S(2)}) async-start(), calls=%async_computation.1 | async-start | bytes 17825792 | tf_op jit(solution)/shard_map/all_gather | solution.py:20
  201.7 127.9 %collective-permute-start = (bf16[2,1024,4096]{2,1,0:T(8,128)(2,1)}, bf16[2,1024,4096]{2,1,0:T(8,128)(2,1)}, u32[]{:S(2)}, u32[]{:S(2)}) collective-permute-start(bf16[2,1024,4096]{2,1,0:T(8,128)(2,1)} %bitcast.53), channel_id=1, source_target_pairs={{0,8},{8,0},{1,9},{9,1},{2,10},{10,2},{3,11},{11,3},{4,12},{12,4},... | collective-permute-start | bytes 50331656 | tf_op jit(solution)/shard_map/ppermute | solution.py:22
  207.8 85.8 %all-to-all-start = ((bf16[128,32,448]{0,2,1:T(8,128)(2,1)}), bf16[128,32,448]{0,2,1:T(8,128)(2,1)}, u32[]{:S(2)}, u32[]{:S(2)}) async-start(bf16[128,32,448]{0,2,1:T(8,128)(2,1)} %bitcast.52), calls=%async_computation | async-start | bytes 7340032 | tf_op jit(solution)/shard_map/all_to_all | solution.py:18
  343.6 86.2 %copy-start.1 = (s32[4]{0:T(128)S(1)}, s32[4]{0:T(128)}, u32[]{:S(2)}) copy-start(s32[4]{0:T(128)} %param.14) | copy-start | bytes 52
  343.6 86.3 %copy-start = (f32[4]{0:T(128)S(1)}, f32[4]{0:T(128)}, u32[]{:S(2)}) copy-start(f32[4]{0:T(128)} %param.13) | copy-start | bytes 52
  432.4 25.0 %copy-start.2 = (f32[4]{0:T(128)}, f32[4]{0:T(128)S(1)}, u32[]{:S(2)}) copy-start(f32[4]{0:T(128)S(1)} %broadcast_divide_fusion) | copy-start | bytes 52
Sparse Core Ops, SparseCore 0:
  10.8 190.8 all-gather.3
